TPU v7x, 512 devices: a whole 4x8x8 slice. The times are simulated.
512 devices in a mesh: section: 8 (over z), kv: 64 (over x, y, core).
Axes of the slice: x: 4, y: 8, z: 8, core: 2. Of those that a mesh axis runs over, the one named last changes fastest.
Arguments:
- held: bfloat16 [8, 128, 8192], P('section', None, 'kv'), may hold values from -6 to 6
- fresh: bfloat16 [1, 128, 8192], P(None, None, 'kv'), may hold values from -6 to 6
- block_starts: int32 [8], replicated, may hold values from 12288 to 24576
- fresh_starts: int32 [1], replicated, may hold values from 12288 to 24576
- norm_gain: float32 [8, 8192], P('section'), may hold values from 0.25 to 1.75
- w_qkv: bfloat16 [8, 8192, 5120], P('section', None, 'kv'), may hold values from -0.0625 to 0.0625
- w_out: bfloat16 [8, 4096, 8192], P('section', None, 'kv'), may hold values from -12 to 12
- cache_keys: bfloat16 [8, 24576, 512], P('section', 'kv'), may hold values from -400 to 400
- cache_values: bfloat16 [8, 24576, 512], P('section', 'kv'), may hold values from -6 to 6
- cache_lengths: int32 [8, 64], P('section', 'kv'), may hold values from 96 to 384, as said below
Outputs:
- produced: bfloat16 [8, 2, 128, 8192], P('section', None, None, 'kv')
Inputs may be any that keep to these rules, and one draw needn't show every extreme that they name: `cache_lengths`: each section has one block filled to 384.
All inputs are finite; a program needn't handle non-finite values.
Results may differ from a plain program's by a relative error of at most 0.017.
The roundings to bfloat16 on the way count: a program that leaves them out, or rounds other values in their place, can miss the bound.
Values may be sent and summed in bfloat16 or wider, within the bound.
No kernel may reach another device: no remote copies, remote signals or barrier semaphores. Data moves between devices by JAX's collectives and lax.ppermute only.
A program may use at most 128 MiB of HBM per device.

v0:
```python
import jax
import jax.numpy as jnp
from jax import lax
from jax.sharding import PartitionSpec as P

HD = 128
HEADS_Q = 32
KV_HEADS = 4


def passed_along(block, axis, distance):
    devices = range(lax.axis_size(axis))
    route = [(i - distance, i) for i in devices if i - distance in devices]
    return lax.ppermute(block, axis, route)


def block_partial(query, key_rows, value_rows, valid):
    row_count = query.shape[0]
    head_count = query.shape[1]
    head_width = query.shape[2]
    group_count = key_rows.shape[1]
    group_size = head_count // group_count
    shaped = jnp.transpose(
        query.reshape(row_count, group_count, group_size, head_width), (1, 0, 2, 3)
    )
    key_major = jnp.transpose(key_rows, (1, 0, 2))
    value_major = jnp.transpose(value_rows, (1, 0, 2))
    allowed = valid[:, None, :]

    def one_group(packed):
        group_query, group_keys, group_values = packed
        scores = jnp.einsum(
            "tgd,id->tgi", group_query, group_keys, preferred_element_type=jnp.float32
        ) * head_width ** (-0.5)
        row_max = jnp.max(jnp.where(allowed, scores, -1e30), axis=2)
        expo = jnp.where(allowed, jnp.exp(scores - row_max[..., None]), 0.0)
        row_sum = jnp.sum(expo, axis=2)
        weights = expo.astype(jnp.bfloat16)
        weighted = jnp.einsum(
            "tgi,id->tgd", weights, group_values, preferred_element_type=jnp.float32
        )
        return (row_max, row_sum, weighted)

    maxima, totals, sums = lax.map(one_group, (shaped, key_major, value_major))
    maxima = jnp.transpose(maxima, (1, 0, 2)).reshape(row_count, head_count)
    totals = jnp.transpose(totals, (1, 0, 2)).reshape(row_count, head_count)
    sums = jnp.transpose(sums, (1, 0, 2, 3)).reshape(row_count, head_count * head_width)
    return (maxima, totals, sums)


def combine_two(left_part, right_part):
    head_count = left_part[0].shape[1]
    row_count = left_part[0].shape[0]
    overall = jnp.maximum(left_part[0], right_part[0])
    left_factor = jnp.exp(left_part[0] - overall)
    right_factor = jnp.exp(right_part[0] - overall)
    total = left_part[1] * left_factor + right_part[1] * right_factor
    left_sum = left_part[2].reshape(row_count, head_count, -1) * left_factor[..., None]
    right_sum = right_part[2].reshape(row_count, head_count, -1) * right_factor[..., None]
    return (overall, total, (left_sum + right_sum).reshape(row_count, -1))


def merge_stack(maxima, totals, sums):
    count = maxima.shape[0]
    row_count = maxima.shape[1]
    head_count = maxima.shape[2]
    overall = jnp.max(maxima, axis=0)
    factor = jnp.exp(maxima - overall)
    total = jnp.sum(totals * factor, axis=0)
    summed = jnp.sum(sums.reshape(count, row_count, head_count, -1) * factor[..., None], axis=0)
    return (summed / total[..., None]).reshape(row_count, -1).astype(jnp.bfloat16)


def on_device(
    held,
    fresh,
    block_starts,
    fresh_starts,
    norm_gain,
    w_qkv,
    w_out,
    cache_keys,
    cache_values,
    cache_lengths,
):
    kv_index = lax.axis_index("kv")
    section_index = lax.axis_index("section")
    tick_count = fresh.shape[0] + 1
    row_count = held.shape[1]
    slot_count = cache_keys.shape[1]
    key_rows = cache_keys[0].reshape(slot_count, KV_HEADS, HD)
    value_rows = cache_values[0].reshape(slot_count, KV_HEADS, HD)
    filled = cache_lengths[0, 0]
    gain = norm_gain[0]
    weight_in = w_qkv[0]
    weight_out = w_out[0]
    slot_ids = jnp.arange(slot_count, dtype=jnp.int32)
    positions = kv_index * slot_count + slot_ids
    row_ids = jnp.arange(row_count, dtype=jnp.int32)
    causal = row_ids[None, :] <= row_ids[:, None]
    current = held[0]
    results = []
    for tick_index in range(tick_count):
        if tick_index > 0:
            passed = passed_along(current, "section", 1)
            current = jnp.where(section_index == 0, fresh[tick_index - 1], passed)
        anchor = section_index - tick_index
        start = jnp.where(
            anchor >= 0,
            block_starts[jnp.maximum(anchor, 0)],
            fresh_starts[jnp.clip(-anchor - 1, 0, tick_count - 2)],
        )
        gathered = lax.all_gather(current, "kv", axis=1, tiled=True)
        wide = gathered.astype(jnp.float32)
        normed = (
            wide * lax.rsqrt(jnp.mean(wide * wide, axis=1, keepdims=True) + 1e-05) * gain
        ).astype(jnp.bfloat16)
        local_cols = jnp.dot(normed, weight_in, preferred_element_type=jnp.float32).astype(
            jnp.bfloat16
        )
        united = lax.all_gather(local_cols, "kv", axis=1, tiled=True)
        query = united[:, : HEADS_Q * HD].reshape(row_count, HEADS_Q, HD)
        new_keys = united[:, HEADS_Q * HD : (HEADS_Q + KV_HEADS) * HD].reshape(
            row_count, KV_HEADS, HD
        )
        new_values = united[:, (HEADS_Q + KV_HEADS) * HD :].reshape(row_count, KV_HEADS, HD)
        usable = (slot_ids < filled) & (positions < start)
        valid = jnp.broadcast_to(usable[None, :], (row_count, slot_count))
        partial_value = block_partial(query, key_rows, value_rows, valid)

        def with_own(parts):
            return combine_two(parts, block_partial(query, new_keys, new_values, causal))

        def without_own(parts):
            return parts

        partial_value = lax.cond(kv_index == 0, with_own, without_own, partial_value)
        received = (
            lax.all_to_all(partial_value[0][None], "kv", split_axis=1, concat_axis=0, tiled=True),
            lax.all_to_all(partial_value[1][None], "kv", split_axis=1, concat_axis=0, tiled=True),
            lax.all_to_all(partial_value[2][None], "kv", split_axis=1, concat_axis=0, tiled=True),
        )
        attended = merge_stack(received[0], received[1], received[2])
        branch = jnp.dot(
            lax.all_gather(attended, "kv", axis=0, tiled=True),
            weight_out,
            preferred_element_type=jnp.float32,
        )
        current = (current.astype(jnp.float32) + branch).astype(jnp.bfloat16)
        results.append(current)
    return jnp.stack(results, 0)[None]


def solution(mesh):
    in_specs = (
        P("section", None, "kv"),
        P(None, None, "kv"),
        P(),
        P(),
        P("section", None),
        P("section", None, "kv"),
        P("section", None, "kv"),
        P("section", "kv", None),
        P("section", "kv", None),
        P("section", "kv"),
    )
    out_specs = P("section", None, None, "kv")
    return jax.shard_map(
        on_device, mesh=mesh, in_specs=in_specs, out_specs=out_specs, check_vma=False
    )
```

profile of v0, /device:TPU:1, one launch (start us, length us, event | category | flops | bytes accessed | tf_op | source)
XLA Modules:
  0.0 792.7 jit_solution(17048475888363732458)
XLA Ops:
  7.3 86.4 %all-gather.16.cloned.1.call-done = bf16[1,128,8192]{2,1,0:T(8,128)(2,1)} async-done(((bf16[1,128,128]{2,1,0:T(8,128)(2,1)}), bf16[1,128,8192]{2,1,0:T(8,128)(2,1)}) %all-gather.16.cloned.1.call-update) | async-done | bytes 2097168 | tf_op jit(solution)/shard_map/all_gather | solution.py:113
  93.7 2.2 fusion.77
  96.0 1.6 fusion.97
  97.9 0.9 copy.78
  99.0 0.9 copy.79
  103.6 75.6 %all-gather.10.cloned.1.call-done = bf16[128,5120]{0,1:T(8,128)(2,1)} async-done(((bf16[128,80]{0,1:T(8,128)(2,1)}), bf16[128,5120]{0,1:T(8,128)(2,1)}) %all-gather.10.cloned.1.call-update) | async-done | bytes 1310736 | tf_op jit(solution)/shard_map/all_gather | solution.py:121
  179.2 1.3 slice.24
  180.6 1.3 copy.75
  182.1 13.5 %while.58 = (s32[]{:T(128)}, f32[4,128,8]{1,2,0:T(8,128)S(1)}, f32[4,128,8]{1,2,0:T(8,128)S(1)}, f32[4,128,8,128]{3,1,2,0:T(8,128)S(1)}, bf16[4,128,8,128]{3,1,2...) while((s32[]{:T(128)}, f32[4,128,8]{1,2,0:T(8,128)S(1)}, ...), condition=%wide.region_4.5_spmd.clone, body=%wide.region_1.4_spmd.clone.sunk | while | flops 204863488 | bytes 5737833 | solution.py:44
  182.1 1.5 select_reduce_fusion.8
  184.1 1.3 fusion.142
  185.5 1.5 select_reduce_fusion.8
  187.5 1.3 fusion.142
  188.9 1.5 select_reduce_fusion.8
  190.9 1.3 fusion.142
  192.2 1.5 select_reduce_fusion.8
  194.2 1.3 fusion.142
  195.6 12.1 %conditional.2 = (f32[128,32]{0,1:T(8,128)S(1)}, f32[128,32]{0,1:T(8,128)S(1)}, f32[128,4096]{1,0:T(8,128)}) conditional(s32[]{:T(128)} %convert_element_type.53, (f32[128,4,8,128]{3,0,2,1:T(8,128)S(1)}, f32[128,32]{0,1:T(8,128)S(1)}, f32[128,32]{0,1:T(8,128)S(1)}) %tuple.192, (bf16[128,4096]{0,1:T(8,128)(2,1)}, bf16[128,5120]{0,1:T(8,128)(2,1)}, ...), branch_computations={%region_5.6_spmd, %region_6.11_spmd} | conditional | flops 69883904 | bytes 51759524 | solution.py:137
  195.6 1.2 copy.80
  196.8 3.0 copy.131
  207.7 0.7 copy.83
  208.4 25.7 %all-to-all-start.2 = ((f32[1,128,32]{2,0,1:T(1,128)}), f32[1,128,32]{2,0,1:T(1,128)S(1)}, u32[]{:S(2)}, u32[]{:S(2)}) async-start(f32[1,128,32]{2,0,1:T(1,128)} %bitcast.73), calls=%async_computation.2 | async-start | bytes 131072 | tf_op jit(solution)/shard_map/all_to_all | solution.py:140
  234.1 0.7 copy.82
  234.8 9.2 %all-to-all-done.2 = f32[1,128,32]{2,0,1:T(1,128)S(1)} async-done(((f32[1,128,32]{2,0,1:T(1,128)}), f32[1,128,32]{2,0,1:T(1,128)S(1)}, u32[]{:S(2)}, u32[]{:S(2)}) %all-to-all-start.2) | async-done | bytes 16416 | tf_op jit(solution)/shard_map/all_to_all | solution.py:140
  244.0 4.4 all-to-all-start.1
  248.4 5.3 broadcast_in_dim.169
  253.8 4.5 all-to-all-done.1
  258.3 5.9 all-to-all-start
  264.9 0.9 multiply_reduce_fusion.3
  265.9 49.5 %all-to-all-done = f32[1,128,4096]{2,0,1:T(1,128)S(1)} async-done(((f32[1,128,4096]{2,0,1:T(1,128)}), f32[1,128,4096]{2,0,1:T(1,128)S(1)}, u32[]{:S(2)}, u32[]{:S(2)}) %all-to-all-start) | async-done | bytes 2097184 | tf_op jit(solution)/shard_map/all_to_all | solution.py:141
  316.0 4.3 multiply_reduce_fusion.1
  321.1 79.2 %all-gather.18.cloned.1.call-done = bf16[64,2,4096]{2,1,0:T(2,128)(2,1)} async-done(((bf16[1,2,4096]{2,1,0:T(2,128)(2,1)}), bf16[64,2,4096]{2,1,0:T(2,128)(2,1)}) %all-gather.18.cloned.1.call-update) | async-done | bytes 1048592 | tf_op jit(solution)/shard_map/all_gather | solution.py:145
  400.3 1.5 reshape.190
  402.2 3.3 collective-permute-start
  405.5 1.0 collective-permute-done
  407.3 78.1 %all-gather.12.cloned.1.call-done = bf16[128,8192]{1,0:T(8,128)(2,1)} async-done(((bf16[128,128]{1,0:T(8,128)(2,1)}), bf16[128,8192]{1,0:T(8,128)(2,1)}) %all-gather.12.cloned.1.call-update) | async-done | bytes 2097168 | tf_op jit(solution)/shard_map/all_gather | solution.py:113
  485.5 2.2 fusion.74
  487.7 1.6 fusion.92
  489.4 81.6 %all-gather.14.cloned.1.call-done = bf16[128,5120]{0,1:T(8,128)(2,1)} async-done(((bf16[128,80]{0,1:T(8,128)(2,1)}), bf16[128,5120]{0,1:T(8,128)(2,1)}) %all-gather.14.cloned.1.call-update) | async-done | bytes 1310736 | tf_op jit(solution)/shard_map/all_gather | solution.py:121
  571.0 1.3 slice.25
  572.3 1.3 copy.84
  573.9 13.5 %while.59 = (s32[]{:T(128)}, f32[4,128,8]{1,2,0:T(8,128)S(1)}, f32[4,128,8]{1,2,0:T(8,128)S(1)}, f32[4,128,8,128]{3,1,2,0:T(8,128)S(1)}, bf16[4,128,8,128]{3,1,2...) while((s32[]{:T(128)}, f32[4,128,8]{1,2,0:T(8,128)S(1)}, ...), condition=%wide.region_18.19_spmd.clone, body=%wide.region_15.18_spmd.clone.sunk | while | flops 204863488 | bytes 5737833 | solution.py:44
  573.9 1.5 select_reduce_fusion.9
  575.9 1.3 fusion.146
  577.3 1.5 select_reduce_fusion.9
  579.3 1.3 fusion.146
  580.6 1.5 select_reduce_fusion.9
  582.6 1.3 fusion.146
  584.0 1.5 select_reduce_fusion.9
  586.0 1.3 fusion.146
  587.4 4.4 conditional.3
  587.4 1.2 copy.87
  588.6 3.0 copy.132
  592.5 24.2 %all-to-all-start.5 = ((f32[1,128,32]{2,0,1:T(1,128)}), f32[1,128,32]{2,0,1:T(1,128)S(1)}, u32[]{:S(2)}, u32[]{:S(2)}) async-start(f32[1,128,32]{2,0,1:T(1,128)} %bitcast.95), calls=%async_computation.5 | async-start | bytes 131072 | tf_op jit(solution)/shard_map/all_to_all | solution.py:140
  616.7 0.7 copy.89
  617.4 9.2 %all-to-all-done.5 = f32[1,128,32]{2,0,1:T(1,128)S(1)} async-done(((f32[1,128,32]{2,0,1:T(1,128)}), f32[1,128,32]{2,0,1:T(1,128)S(1)}, u32[]{:S(2)}, u32[]{:S(2)}) %all-to-all-start.5) | async-done | bytes 16416 | tf_op jit(solution)/shard_map/all_to_all | solution.py:140
  626.6 4.4 all-to-all-start.4
  631.0 5.3 broadcast_in_dim.172
  636.3 4.5 all-to-all-done.4
  640.9 5.9 all-to-all-start.3
  647.1 50.9 %all-to-all-done.3 = f32[1,128,4096]{2,0,1:T(1,128)S(1)} async-done(((f32[1,128,4096]{2,0,1:T(1,128)}), f32[1,128,4096]{2,0,1:T(1,128)S(1)}, u32[]{:S(2)}, u32[]{:S(2)}) %all-to-all-start.3) | async-done | bytes 2097184 | tf_op jit(solution)/shard_map/all_to_all | solution.py:141
  698.6 4.3 multiply_reduce_fusion
  703.6 79.3 %all-gather.20.cloned.1.call-done = bf16[64,2,4096]{2,1,0:T(2,128)(2,1)} async-done(((bf16[1,2,4096]{2,1,0:T(2,128)(2,1)}), bf16[64,2,4096]{2,1,0:T(2,128)(2,1)}) %all-gather.20.cloned.1.call-update) | async-done | bytes 1048592 | tf_op jit(solution)/shard_map/all_gather | solution.py:145
  782.9 1.5 reshape.192
  (93 shorter events, 13.9 us)
Async XLA Ops:
  6.5 89.4 %copy-start = (bf16[1,8192,80]{1,2,0:T(8,128)(2,1)S(1)}, bf16[1,8192,80]{1,2,0:T(8,128)(2,1)}, u32[]{:S(2)}) copy-start(bf16[1,8192,80]{1,2,0:T(8,128)(2,1)} %param.27) | copy-start | bytes 3932164
  6.5 89.4 %copy-start.27 = (f32[1,8192]{1,0:T(1,128)S(1)}, f32[1,8192]{1,0:T(1,128)}, u32[]{:S(2)}) copy-start(f32[1,8192]{1,0:T(1,128)} %param.26) | copy-start | bytes 98308
  6.5 87.1 %all-gather.16.cloned.1.call-start = ((), (), s32[]{:S(2)}) async-start(), calls=%async_computation.9 | async-start | bytes 2129920 | tf_op jit(solution)/shard_map/all_gather | solution.py:113
  7.3 172.0 %all-gather.10.cloned.1.call-start = ((), (), s32[]{:S(2)}) async-start(), calls=%async_computation.6 | async-start | bytes 1331200 | tf_op jit(solution)/shard_map/all_gather | solution.py:121
  93.7 2.3 copy-start.9
  95.9 1.7 copy-start.13
  95.9 2.9 copy-start.14
  97.6 3.7 copy-start.26
  180.5 1.3 copy-start.2
  208.4 35.6 %all-to-all-start.2 = ((f32[1,128,32]{2,0,1:T(1,128)}), f32[1,128,32]{2,0,1:T(1,128)S(1)}, u32[]{:S(2)}, u32[]{:S(2)}) async-start(f32[1,128,32]{2,0,1:T(1,128)} %bitcast.73), calls=%async_computation.2 | async-start | bytes 131072 | tf_op jit(solution)/shard_map/all_to_all | solution.py:140
  244.0 9.8 %copy-start.16 = (f32[1,128,32]{2,0,1:T(1,128)}, f32[1,128,32]{2,0,1:T(1,128)S(1)}, u32[]{:S(2)}) copy-start(f32[1,128,32]{2,0,1:T(1,128)S(1)} %all-to-all-done.2) | copy-start | bytes 49156
  244.0 14.3 %all-to-all-start.1 = ((f32[1,128,32]{2,0,1:T(1,128)}), f32[1,128,32]{2,0,1:T(1,128)S(1)}, u32[]{:S(2)}, u32[]{:S(2)}) async-start(f32[1,128,32]{2,0,1:T(1,128)} %bitcast.70), calls=%async_computation.1 | async-start | bytes 131072 | tf_op jit(solution)/shard_map/all_to_all | solution.py:139
  258.3 57.1 %all-to-all-start = ((f32[1,128,4096]{2,0,1:T(1,128)}), f32[1,128,4096]{2,0,1:T(1,128)S(1)}, u32[]{:S(2)}, u32[]{:S(2)}) async-start(f32[1,128,4096]{2,0,1:T(1,128)} %broadcast_in_dim.169), calls=%async_computation | async-start | bytes 4194304 | tf_op jit(solution)/shard_map/all_to_all | solution.py:141
  264.2 136.0 %all-gather.18.cloned.1.call-start = ((), (), s32[]{:S(2)}) async-start(), calls=%async_computation.10 | async-start | bytes 1064960 | tf_op jit(solution)/shard_map/all_gather | solution.py:145
  320.3 81.4 %copy-start.7 = (bf16[1,4096,128]{2,1,0:T(8,128)(2,1)S(1)}, bf16[1,4096,128]{2,1,0:T(8,128)(2,1)}, u32[]{:S(2)}) copy-start(bf16[1,4096,128]{2,1,0:T(8,128)(2,1)} %param.28) | copy-start | bytes 3145732
  320.3 81.4 %copy-start.21 = (bf16[1,128,128]{2,1,0:T(8,128)(2,1)S(1)}, bf16[1,128,128]{2,1,0:T(8,128)(2,1)}, u32[]{:S(2)}) copy-start(bf16[1,128,128]{2,1,0:T(8,128)(2,1)} %param.22) | copy-start | bytes 98308
  321.0 85.5 %copy-start.25 = (bf16[1,128,128]{2,1,0:T(8,128)(2,1)S(1)}, bf16[1,128,128]{2,1,0:T(8,128)(2,1)}, u32[]{:S(2)}) copy-start(bf16[1,128,128]{2,1,0:T(8,128)(2,1)} %param.23) | copy-start | bytes 98308
  321.0 164.5 %all-gather.12.cloned.1.call-start = ((), (), s32[]{:S(2)}) async-start(), calls=%async_computation.7 | async-start | bytes 2129920 | tf_op jit(solution)/shard_map/all_gather | solution.py:113
  401.7 86.0 %copy-start.28 = (f32[1,8192]{1,0:T(1,128)S(1)}, f32[1,8192]{1,0:T(1,128)}, u32[]{:S(2)}) copy-start(f32[1,8192]{1,0:T(1,128)} %param.26) | copy-start | bytes 98308
  402.2 87.2 %copy-start.22 = (bf16[128,128]{1,0:T(8,128)(2,1)}, bf16[128,128]{1,0:T(8,128)(2,1)S(1)}, u32[]{:S(2)}) copy-start(bf16[128,128]{1,0:T(8,128)(2,1)S(1)} %fusion.91) | copy-start | bytes 98308
  402.2 4.3 collective-permute-start
  407.1 163.9 %all-gather.14.cloned.1.call-start = ((), (), s32[]{:S(2)}) async-start(), calls=%async_computation.8 | async-start | bytes 1331200 | tf_op jit(solution)/shard_map/all_gather | solution.py:121
  485.5 2.3 copy-start.10
  572.3 1.6 copy-start.24
  592.5 34.1 %all-to-all-start.5 = ((f32[1,128,32]{2,0,1:T(1,128)}), f32[1,128,32]{2,0,1:T(1,128)S(1)}, u32[]{:S(2)}, u32[]{:S(2)}) async-start(f32[1,128,32]{2,0,1:T(1,128)} %bitcast.95), calls=%async_computation.5 | async-start | bytes 131072 | tf_op jit(solution)/shard_map/all_to_all | solution.py:140
  626.6 14.3 %all-to-all-start.4 = ((f32[1,128,32]{2,0,1:T(1,128)}), f32[1,128,32]{2,0,1:T(1,128)S(1)}, u32[]{:S(2)}, u32[]{:S(2)}) async-start(f32[1,128,32]{2,0,1:T(1,128)} %bitcast.92), calls=%async_computation.4 | async-start | bytes 131072 | tf_op jit(solution)/shard_map/all_to_all | solution.py:139
  640.9 57.1 %all-to-all-start.3 = ((f32[1,128,4096]{2,0,1:T(1,128)}), f32[1,128,4096]{2,0,1:T(1,128)S(1)}, u32[]{:S(2)}, u32[]{:S(2)}) async-start(f32[1,128,4096]{2,0,1:T(1,128)} %broadcast_in_dim.172), calls=%async_computation.3 | async-start | bytes 4194304 | tf_op jit(solution)/shard_map/all_to_all | solution.py:141
  646.8 136.1 %all-gather.20.cloned.1.call-start = ((), (), s32[]{:S(2)}) async-start(), calls=%async_computation.11 | async-start | bytes 1064960 | tf_op jit(solution)/shard_map/all_gather | solution.py:145
  702.9 81.5 %copy-start.8 = (bf16[1,4096,128]{2,1,0:T(8,128)(2,1)S(1)}, bf16[1,4096,128]{2,1,0:T(8,128)(2,1)}, u32[]{:S(2)}) copy-start(bf16[1,4096,128]{2,1,0:T(8,128)(2,1)} %param.28) | copy-start | bytes 3145732
  702.9 81.5 %copy-start.15 = (bf16[128,128]{1,0:T(8,128)(2,1)S(1)}, bf16[128,128]{1,0:T(8,128)(2,1)}, u32[]{:S(2)}) copy-start(bf16[128,128]{1,0:T(8,128)(2,1)} %bitcast_select_fusion) | copy-start | bytes 98308
  703.6 81.2 %copy-start.23 = (bf16[128,128]{1,0:T(8,128)(2,1)S(1)}, bf16[128,128]{1,0:T(8,128)(2,1)}, u32[]{:S(2)}) copy-start(bf16[128,128]{1,0:T(8,128)(2,1)} %copy-done.22) | copy-start | bytes 98308
  703.6 81.8 %copy-start.1 = (bf16[1,8192,80]{1,2,0:T(8,128)(2,1)S(1)}, bf16[1,8192,80]{1,2,0:T(8,128)(2,1)}, u32[]{:S(2)}) copy-start(bf16[1,8192,80]{1,2,0:T(8,128)(2,1)} %param.27) | copy-start | bytes 3932164
Sparse Core Ops, SparseCore 0:
  10.5 83.1 all-gather.15
  97.7 81.4 all-gather.9
  321.1 79.0 all-gather.17
  407.2 78.1 all-gather.11
  489.5 81.4 all-gather.13
  703.7 79.1 all-gather.19
where the time goes:
time: 800 us; the launch traced here: 793 us
  waiting for transfers between devices  610 us (76%)
  starting transfers between devices  74.2 us (9%)
  local copies, waits for them, and re-layouts  35 us (4%)
  matrix products  26.5 us (3%)
  other arithmetic  22.1 us (3%)
  between operations  16.8 us (2%)
  loops' own time  8.38 us (1%)
    all_gather x2, waiting for transfers between devices, on_device(): gathered = lax.all_gather(current, 'kv', axis=1, tiled=True)  164 us
    all_gather x2, waiting for transfers between devices, on_device(): lax.all_gather(attended, 'kv', axis=0, tiled=True)  158 us
    all_gather x2, waiting for transfers between devices, on_device(): united = lax.all_gather(local_cols, 'kv', axis=1, tiled=True)  157 us
    all_to_all x2, waiting for transfers between devices, on_device(): lax.all_to_all(partial_value[2][None], 'kv', split_axis=1, concat_axis=0,...  100 us
    all_to_all x2, starting transfers between devices, on_device(): lax.all_to_all(partial_value[1][None], 'kv', split_axis=1, concat_axis=0,...  49.9 us
    all_to_all x2, waiting for transfers between devices, on_device(): lax.all_to_all(partial_value[1][None], 'kv', split_axis=1, concat_axis=0,...  18.3 us
  transfers between devices with their start and end apart: 13, of which 13 were waited for; matrix products, arithmetic and copies ran while one was open for 2% of the time, Pallas kernels for 0%

commit v1 on v0

v1 whole, which is shorter than its diff:
```python
import jax
import jax.numpy as jnp
from jax import lax
from jax.sharding import PartitionSpec as P

HD = 128
HEADS_Q = 32
KV_HEADS = 4
GROUP = HEADS_Q // KV_HEADS
EMPTY = -1e30


def passed_along(block, axis, distance):
    devices = range(lax.axis_size(axis))
    route = [(i - distance, i) for i in devices if i - distance in devices]
    return lax.ppermute(block, axis, route)


def split3(value):
    hi = lax.reduce_precision(value, exponent_bits=8, mantissa_bits=7)
    rest = value - hi
    mid = lax.reduce_precision(rest, exponent_bits=8, mantissa_bits=7)
    lo = rest - mid
    return [part.astype(jnp.bfloat16) for part in (hi, mid, lo)]


def softmax_block(scores, valid, values):
    top = jnp.max(jnp.where(valid, scores, EMPTY), axis=-1)
    expo = jnp.where(valid, jnp.exp(scores - top[..., None]), 0.0)
    total = jnp.sum(expo, axis=-1)
    weighted = jnp.einsum(
        "kni,kid->knd", expo.astype(jnp.bfloat16), values, preferred_element_type=jnp.float32
    )
    filled = total > 0
    safe = jnp.where(filled, total, 1.0)
    out = jnp.where(filled[..., None], weighted / safe[..., None], 0.0)
    lse = jnp.where(filled, top + jnp.log(safe), EMPTY)
    return out, lse


def on_device(
    held,
    fresh,
    block_starts,
    fresh_starts,
    norm_gain,
    w_qkv,
    w_out,
    cache_keys,
    cache_values,
    cache_lengths,
):
    kv_index = lax.axis_index("kv")
    kv_count = lax.axis_size("kv")
    section_index = lax.axis_index("section")
    tick_count = fresh.shape[0] + 1
    row_count = held.shape[1]
    own_rows = row_count // kv_count
    slot_count = cache_keys.shape[1]
    scale = HD ** (-0.5)
    key_major = jnp.transpose(cache_keys[0].reshape(slot_count, KV_HEADS, HD), (1, 0, 2))
    value_major = jnp.transpose(cache_values[0].reshape(slot_count, KV_HEADS, HD), (1, 0, 2))
    filled = cache_lengths[0, 0]
    gain = norm_gain[0]
    weight_in = w_qkv[0]
    weight_out = w_out[0]
    slot_ids = jnp.arange(slot_count, dtype=jnp.int32)
    positions = kv_index * slot_count + slot_ids
    mine = kv_index * own_rows + jnp.arange(own_rows, dtype=jnp.int32)
    causal = jnp.arange(row_count, dtype=jnp.int32)[None, :] <= mine[:, None]
    current = held[0]
    results = []
    for tick_index in range(tick_count):
        if tick_index > 0:
            passed = passed_along(current, "section", 1)
            current = jnp.where(section_index == 0, fresh[tick_index - 1], passed)
        anchor = section_index - tick_index
        start = jnp.where(
            anchor >= 0,
            block_starts[jnp.maximum(anchor, 0)],
            fresh_starts[jnp.clip(-anchor - 1, 0, tick_count - 2)],
        )
        gathered = lax.all_gather(current, "kv", axis=1, tiled=True)
        wide = gathered.astype(jnp.float32)
        normed = (
            wide * lax.rsqrt(jnp.mean(wide * wide, axis=1, keepdims=True) + 1e-05) * gain
        ).astype(jnp.bfloat16)
        local_cols = jnp.dot(normed, weight_in, preferred_element_type=jnp.float32).astype(
            jnp.bfloat16
        )
        united = lax.all_gather(local_cols, "kv", axis=1, tiled=True)
        query = united[:, : HEADS_Q * HD].reshape(row_count, KV_HEADS, GROUP, HD)
        new_keys = united[:, HEADS_Q * HD : (HEADS_Q + KV_HEADS) * HD].reshape(
            row_count, KV_HEADS, HD
        )
        new_values = united[:, (HEADS_Q + KV_HEADS) * HD :].reshape(row_count, KV_HEADS, HD)

        grouped = jnp.transpose(query, (1, 2, 0, 3)).reshape(KV_HEADS, GROUP * row_count, HD)
        scores = jnp.einsum(
            "knd,kid->kni", grouped, key_major, preferred_element_type=jnp.float32
        ) * scale
        usable = (slot_ids < filled) & (positions < start)
        out, lse = softmax_block(scores, usable[None, None, :], value_major)
        out = jnp.transpose(out.reshape(KV_HEADS, GROUP, row_count, HD), (2, 0, 1, 3))
        out = out.reshape(row_count, HEADS_Q * HD)
        lse = jnp.transpose(lse.reshape(KV_HEADS, GROUP, row_count), (2, 0, 1))
        lse = lse.reshape(row_count, HEADS_Q)
        packed = jnp.concatenate([out.astype(jnp.bfloat16)] + split3(lse), axis=1)
        received = lax.all_to_all(
            packed.reshape(kv_count, own_rows, -1), "kv", split_axis=0, concat_axis=0, tiled=True
        )
        got_out = received[:, :, : HEADS_Q * HD].astype(jnp.float32)
        got_lse = (
            received[:, :, HEADS_Q * HD : HEADS_Q * HD + HEADS_Q].astype(jnp.float32)
            + received[:, :, HEADS_Q * HD + HEADS_Q : HEADS_Q * HD + 2 * HEADS_Q].astype(jnp.float32)
            + received[:, :, HEADS_Q * HD + 2 * HEADS_Q :].astype(jnp.float32)
        )

        my_query = lax.dynamic_slice_in_dim(query, kv_index * own_rows, own_rows, axis=0)
        my_grouped = jnp.transpose(my_query, (1, 2, 0, 3)).reshape(KV_HEADS, GROUP * own_rows, HD)
        own_scores = jnp.einsum(
            "knd,ikd->kni", my_grouped, new_keys, preferred_element_type=jnp.float32
        ) * scale
        own_valid = jnp.broadcast_to(causal[None, None], (1, GROUP, own_rows, row_count)).reshape(
            1, GROUP * own_rows, row_count
        )
        own_out, own_lse = softmax_block(
            own_scores, own_valid, jnp.transpose(new_values, (1, 0, 2))
        )
        own_out = jnp.transpose(own_out.reshape(KV_HEADS, GROUP, own_rows, HD), (2, 0, 1, 3))
        own_out = own_out.reshape(1, own_rows, HEADS_Q * HD)
        own_lse = jnp.transpose(own_lse.reshape(KV_HEADS, GROUP, own_rows), (2, 0, 1))
        own_lse = own_lse.reshape(1, own_rows, HEADS_Q)

        all_out = jnp.concatenate([got_out, own_out], 0)
        all_lse = jnp.concatenate([got_lse, own_lse], 0)
        overall = jnp.max(all_lse, axis=0)
        factor = jnp.exp(all_lse - overall)
        total = jnp.sum(factor, axis=0)
        summed = jnp.sum(
            all_out.reshape(kv_count + 1, own_rows, HEADS_Q, HD) * factor[..., None], axis=0
        )
        attended = (summed / total[..., None]).reshape(own_rows, HEADS_Q * HD).astype(jnp.bfloat16)
        branch = jnp.dot(
            lax.all_gather(attended, "kv", axis=0, tiled=True),
            weight_out,
            preferred_element_type=jnp.float32,
        )
        current = (current.astype(jnp.float32) + branch).astype(jnp.bfloat16)
        results.append(current)
    return jnp.stack(results, 0)[None]


def solution(mesh):
    in_specs = (
        P("section", None, "kv"),
        P(None, None, "kv"),
        P(),
        P(),
        P("section", None),
        P("section", None, "kv"),
        P("section", None, "kv"),
        P("section", "kv", None),
        P("section", "kv", None),
        P("section", "kv"),
    )
    out_specs = P("section", None, None, "kv")
    return jax.shard_map(
        on_device, mesh=mesh, in_specs=in_specs, out_specs=out_specs, check_vma=False
    )
```

time: 800 us -> 659 us (0.82)
  waiting for transfers between devices: 610 us -> 531 us
  starting transfers between devices: 74.2 us -> 17.7 us
  local copies, waits for them, and re-layouts: 35 us -> 56.8 us
  matrix products: 26.5 us -> 17.7 us
  loops' own time: 8.38 us -> 0 us
    all_to_all x6 -> x2, waiting for transfers between devices: 128 us -> 47.4 us  [on_device(): lax.all_to_all(packed.reshape(kv_count, own_rows, -1), 'kv', split_axis=0...]
    all_to_all x6 -> x2, starting transfers between devices: 70.5 us -> 13.7 us  [on_device(): lax.all_to_all(packed.reshape(kv_count, own_rows, -1), 'kv', split_axis=0...]
    concatenate x0 -> x6, local copies, waits for them, and re-layouts: none -> 16 us  [the longest x2 9.77 us: on_device(): packed = jnp.concatenate([out.astype(jnp.bfloat16)] + split3(lse), axis=1)]
    dot_general x16 -> x8, matrix products: 22.4 us -> 10.5 us  [the longest x4 5.91 us: softmax_block(): jnp.einsum('kni,kid->knd', expo.astype(jnp.bfloat16), values, preferred_e...]
    broadcast_in_dim x2, local copies, waits for them, and re-layouts: 10.7 us -> 0.03 us  [on_device(): jnp.broadcast_to(causal[None, None], (1, GROUP, own_rows, row_count))]
    transpose x0 -> x10, local copies, waits for them, and re-layouts: none -> 9.12 us  [the longest x4 5.94 us: on_device(): jnp.transpose(my_query, (1, 2, 0, 3))]
    reduce_sum x12 -> x8, other arithmetic: 13.8 us -> 4.79 us  [the longest x4 3.01 us: softmax_block(): total = jnp.sum(expo, axis=-1)]
    cond x6 -> x0, local copies, waits for them, and re-layouts: 8.86 us -> none
  transfers between devices with their start and end apart: 13 -> 9, of which waited for: 13 -> 9; matrix products, arithmetic and copies ran while one was open for 2% -> 2% of each run, Pallas kernels for 0% -> 0%
where the time goes in v1:
time: 659 us; the launch traced here: 657 us
  waiting for transfers between devices  531 us (81%)
  local copies, waits for them, and re-layouts  56.8 us (9%)
  starting transfers between devices  17.7 us (3%)
  matrix products  17.7 us (3%)
  other arithmetic  17.4 us (3%)
  between operations  16.6 us (3%)
    all_gather x2, waiting for transfers between devices, on_device(): gathered = lax.all_gather(current, 'kv', axis=1, tiled=True)  165 us
    all_gather x2, waiting for transfers between devices, on_device(): lax.all_gather(attended, 'kv', axis=0, tiled=True)  159 us
    all_gather x2, waiting for transfers between devices, on_device(): united = lax.all_gather(local_cols, 'kv', axis=1, tiled=True)  158 us
    all_to_all x2, waiting for transfers between devices, on_device(): lax.all_to_all(packed.reshape(kv_count, own_rows, -1), 'kv', split_axis=0...  47.4 us
    all_to_all x2, starting transfers between devices, on_device(): lax.all_to_all(packed.reshape(kv_count, own_rows, -1), 'kv', split_axis=0...  13.7 us
  transfers between devices with their start and end apart: 9, of which 9 were waited for; matrix products, arithmetic and copies ran while one was open for 2% of the time, Pallas kernels for 0%

profile of v1, /device:TPU:1, one launch (start us, length us, event | category | flops | bytes accessed | tf_op | source)
XLA Modules:
  0.0 657.5 jit_solution(9400813591269261089)
XLA Ops:
  6.5 0.7 all-gather.16.cloned.1.call-update
  7.3 86.4 %all-gather.16.cloned.1.call-done = bf16[1,128,8192]{2,1,0:T(8,128)(2,1)} async-done(((bf16[1,128,128]{2,1,0:T(8,128)(2,1)}), bf16[1,128,8192]{2,1,0:T(8,128)(2,1)}) %all-gather.16.cloned.1.call-update) | async-done | bytes 2097168 | tf_op jit(solution)/shard_map/all_gather | solution.py:83
  93.7 2.1 fusion.7
  95.8 3.2 fusion.43
  100.3 0.8 reshape_squeeze.6
  101.2 0.8 reshape_squeeze.7
  103.9 76.7 %all-gather.10.cloned.1.call-done = bf16[128,5120]{0,1:T(8,128)(2,1)} async-done(((bf16[128,80]{0,1:T(8,128)(2,1)}), bf16[128,5120]{0,1:T(8,128)(2,1)}) %all-gather.10.cloned.1.call-update) | async-done | bytes 1310736 | tf_op jit(solution)/shard_map/all_gather | solution.py:91
  180.7 1.3 slice.56
  181.9 0.7 copy.197
  182.6 2.1 select_reduce_fusion.1
  184.7 1.3 fusion.1
  186.1 2.7 select_convert_fusion.1
  188.8 1.7 copy.286
  190.5 1.3 convert_element_type.132
  191.8 0.8 copy.202
  192.7 1.1 reshape.250
  194.2 4.9 concatenate.46
  199.1 6.8 %all-to-all-start = ((bf16[64,2,4192]{2,1,0:T(2,128)(2,1)}), bf16[64,2,4192]{2,1,0:T(2,128)(2,1)S(1)}, u32[]{:S(2)}, u32[]{:S(2)}) async-start(bf16[64,2,4192]{2,1,0:T(2,128)(2,1)} %concatenate.46), calls=%async_computation | async-start | bytes 2162688 | tf_op jit(solution)/shard_map/all_to_all | solution.py:109
  206.3 1.4 dynamic-slice_bitcast_fusion.1
  207.7 1.6 copy.208
  209.3 1.0 fusion.113
  211.5 23.7 %all-to-all-done = bf16[64,2,4192]{2,1,0:T(2,128)(2,1)S(1)} async-done(((bf16[64,2,4192]{2,1,0:T(2,128)(2,1)}), bf16[64,2,4192]{2,1,0:T(2,128)(2,1)S(1)}, u32[]{:S(2)}, u32[]{:S(2)}) %all-to-all-start) | async-done | bytes 1073184 | tf_op jit(solution)/shard_map/all_to_all | solution.py:109
  235.2 1.0 copy-done.1
  236.2 2.5 slice_convert_fusion.1
  238.7 3.1 reshape.264
  241.8 1.7 fusion.115
  243.5 1.4 copy.249
  244.9 0.7 copy.248
  245.7 0.8 fusion.111
  246.8 0.7 fusion.22
  248.4 79.6 %all-gather.18.cloned.1.call-done = bf16[64,2,4096]{2,1,0:T(2,128)(2,1)} async-done(((bf16[1,2,4096]{2,1,0:T(2,128)(2,1)}), bf16[64,2,4096]{2,1,0:T(2,128)(2,1)}) %all-gather.18.cloned.1.call-update) | async-done | bytes 1048592 | tf_op jit(solution)/shard_map/all_gather | solution.py:145
  327.9 1.5 reshape.270
  329.9 3.4 collective-permute-start
  333.3 1.0 collective-permute-done
  335.0 78.3 %all-gather.12.cloned.1.call-done = bf16[128,8192]{1,0:T(8,128)(2,1)} async-done(((bf16[128,128]{1,0:T(8,128)(2,1)}), bf16[128,8192]{1,0:T(8,128)(2,1)}) %all-gather.12.cloned.1.call-update) | async-done | bytes 2097168 | tf_op jit(solution)/shard_map/all_gather | solution.py:83
  413.3 2.1 fusion.4
  415.4 3.1 fusion.38
  418.5 81.6 %all-gather.14.cloned.1.call-done = bf16[128,5120]{0,1:T(8,128)(2,1)} async-done(((bf16[128,80]{0,1:T(8,128)(2,1)}), bf16[128,5120]{0,1:T(8,128)(2,1)}) %all-gather.14.cloned.1.call-update) | async-done | bytes 1310736 | tf_op jit(solution)/shard_map/all_gather | solution.py:91
  500.2 1.3 slice.63
  501.5 0.7 copy.221
  502.1 2.1 select_reduce_fusion
  504.2 1.3 fusion.3
  505.6 2.7 select_convert_fusion
  508.4 1.7 copy.285
  510.0 1.3 convert_element_type.151
  511.4 0.8 copy.224
  512.2 1.1 reshape.258
  513.8 4.9 concatenate.53
  518.6 6.8 %all-to-all-start.1 = ((bf16[64,2,4192]{2,1,0:T(2,128)(2,1)}), bf16[64,2,4192]{2,1,0:T(2,128)(2,1)S(1)}, u32[]{:S(2)}, u32[]{:S(2)}) async-start(bf16[64,2,4192]{2,1,0:T(2,128)(2,1)} %concatenate.53), calls=%async_computation.1 | async-start | bytes 2162688 | tf_op jit(solution)/shard_map/all_to_all | solution.py:109
  525.8 1.4 dynamic-slice_bitcast_fusion
  527.1 1.6 copy.230
  528.7 1.0 fusion.112
  531.0 23.7 %all-to-all-done.1 = bf16[64,2,4192]{2,1,0:T(2,128)(2,1)S(1)} async-done(((bf16[64,2,4192]{2,1,0:T(2,128)(2,1)}), bf16[64,2,4192]{2,1,0:T(2,128)(2,1)S(1)}, u32[]{:S(2)}, u32[]{:S(2)}) %all-to-all-start.1) | async-done | bytes 1073184 | tf_op jit(solution)/shard_map/all_to_all | solution.py:109
  554.7 1.0 copy-done.2
  555.7 2.5 slice_convert_fusion
  558.2 3.1 reshape.265
  561.3 1.7 fusion.114
  563.0 1.4 copy.252
  564.4 0.7 copy.251
  565.1 0.7 copy.250
  565.8 0.8 fusion.108
  567.0 0.7 fusion.23
  568.4 79.6 %all-gather.20.cloned.1.call-done = bf16[64,2,4096]{2,1,0:T(2,128)(2,1)} async-done(((bf16[1,2,4096]{2,1,0:T(2,128)(2,1)}), bf16[64,2,4096]{2,1,0:T(2,128)(2,1)}) %all-gather.20.cloned.1.call-update) | async-done | bytes 1048592 | tf_op jit(solution)/shard_map/all_gather | solution.py:145
  648.1 1.5 reshape.272
  (108 shorter events, 9.0 us)
Async XLA Ops:
  6.5 89.2 %copy-start = (bf16[1,8192,80]{1,2,0:T(8,128)(2,1)S(1)}, bf16[1,8192,80]{1,2,0:T(8,128)(2,1)}, u32[]{:S(2)}) copy-start(bf16[1,8192,80]{1,2,0:T(8,128)(2,1)} %param.15) | copy-start | bytes 3932164
  6.5 89.2 %copy-start.15 = (f32[1,8192]{1,0:T(1,128)S(1)}, f32[1,8192]{1,0:T(1,128)}, u32[]{:S(2)}) copy-start(f32[1,8192]{1,0:T(1,128)} %param.14) | copy-start | bytes 98308
  6.5 87.1 %all-gather.16.cloned.1.call-start = ((), (), s32[]{:S(2)}) async-start(), calls=%async_computation.5 | async-start | bytes 2129920 | tf_op jit(solution)/shard_map/all_gather | solution.py:83
  7.3 173.4 %all-gather.10.cloned.1.call-start = ((), (), s32[]{:S(2)}) async-start(), calls=%async_computation.2 | async-start | bytes 1331200 | tf_op jit(solution)/shard_map/all_gather | solution.py:91
  95.8 4.6 copy-start.5
  95.8 5.4 copy-start.6
  95.8 6.2 copy-start.14
  184.7 1.4 copy-start.7
  199.1 36.1 %all-to-all-start = ((bf16[64,2,4192]{2,1,0:T(2,128)(2,1)}), bf16[64,2,4192]{2,1,0:T(2,128)(2,1)S(1)}, u32[]{:S(2)}, u32[]{:S(2)}) async-start(bf16[64,2,4192]{2,1,0:T(2,128)(2,1)} %concatenate.46), calls=%async_computation | async-start | bytes 2162688 | tf_op jit(solution)/shard_map/all_to_all | solution.py:109
  206.0 122.0 %all-gather.18.cloned.1.call-start = ((), (), s32[]{:S(2)}) async-start(), calls=%async_computation.6 | async-start | bytes 1064960 | tf_op jit(solution)/shard_map/all_gather | solution.py:145
  235.2 1.0 copy-start.1
  246.8 82.6 %copy-start.10 = (bf16[1,128,128]{2,1,0:T(8,128)(2,1)S(1)}, bf16[1,128,128]{2,1,0:T(8,128)(2,1)}, u32[]{:S(2)}) copy-start(bf16[1,128,128]{2,1,0:T(8,128)(2,1)} %param.10) | copy-start | bytes 98308
  247.6 81.9 %copy-start.3 = (bf16[1,4096,128]{2,1,0:T(8,128)(2,1)S(1)}, bf16[1,4096,128]{2,1,0:T(8,128)(2,1)}, u32[]{:S(2)}) copy-start(bf16[1,4096,128]{2,1,0:T(8,128)(2,1)} %param.16) | copy-start | bytes 3145732
  248.3 86.0 %copy-start.13 = (bf16[1,128,128]{2,1,0:T(8,128)(2,1)S(1)}, bf16[1,128,128]{2,1,0:T(8,128)(2,1)}, u32[]{:S(2)}) copy-start(bf16[1,128,128]{2,1,0:T(8,128)(2,1)} %param.11) | copy-start | bytes 98308
  248.3 165.0 %all-gather.12.cloned.1.call-start = ((), (), s32[]{:S(2)}) async-start(), calls=%async_computation.3 | async-start | bytes 2129920 | tf_op jit(solution)/shard_map/all_gather | solution.py:83
  329.9 88.7 %copy-start.11 = (bf16[128,128]{1,0:T(8,128)(2,1)}, bf16[128,128]{1,0:T(8,128)(2,1)S(1)}, u32[]{:S(2)}) copy-start(bf16[128,128]{1,0:T(8,128)(2,1)S(1)} %fusion.35) | copy-start | bytes 98308
  329.9 85.5 %copy-start.16 = (f32[1,8192]{1,0:T(1,128)S(1)}, f32[1,8192]{1,0:T(1,128)}, u32[]{:S(2)}) copy-start(f32[1,8192]{1,0:T(1,128)} %param.14) | copy-start | bytes 98308
  329.9 4.4 collective-permute-start
  335.0 165.2 %all-gather.14.cloned.1.call-start = ((), (), s32[]{:S(2)}) async-start(), calls=%async_computation.4 | async-start | bytes 1331200 | tf_op jit(solution)/shard_map/all_gather | solution.py:91
  504.2 1.4 copy-start.8
  518.6 36.1 %all-to-all-start.1 = ((bf16[64,2,4192]{2,1,0:T(2,128)(2,1)}), bf16[64,2,4192]{2,1,0:T(2,128)(2,1)S(1)}, u32[]{:S(2)}, u32[]{:S(2)}) async-start(bf16[64,2,4192]{2,1,0:T(2,128)(2,1)} %concatenate.53), calls=%async_computation.1 | async-start | bytes 2162688 | tf_op jit(solution)/shard_map/all_to_all | solution.py:109
  525.5 122.6 %all-gather.20.cloned.1.call-start = ((), (), s32[]{:S(2)}) async-start(), calls=%async_computation.7 | async-start | bytes 1064960 | tf_op jit(solution)/shard_map/all_gather | solution.py:145
  554.7 1.0 copy-start.2
  567.0 82.6 %copy-start.9 = (bf16[128,128]{1,0:T(8,128)(2,1)S(1)}, bf16[128,128]{1,0:T(8,128)(2,1)}, u32[]{:S(2)}) copy-start(bf16[128,128]{1,0:T(8,128)(2,1)} %bitcast_select_fusion) | copy-start | bytes 98308
  567.7 81.9 %copy-start.4 = (bf16[1,4096,128]{2,1,0:T(8,128)(2,1)S(1)}, bf16[1,4096,128]{2,1,0:T(8,128)(2,1)}, u32[]{:S(2)}) copy-start(bf16[1,4096,128]{2,1,0:T(8,128)(2,1)} %param.16) | copy-start | bytes 3145732
  568.4 81.6 %copy-start.12 = (bf16[128,128]{1,0:T(8,128)(2,1)S(1)}, bf16[128,128]{1,0:T(8,128)(2,1)}, u32[]{:S(2)}) copy-start(bf16[128,128]{1,0:T(8,128)(2,1)} %copy-done.11) | copy-start | bytes 98308
Sparse Core Ops, SparseCore 0:
  10.5 83.1 all-gather.15
  99.1 81.4 all-gather.9
  248.4 79.4 all-gather.17
  335.1 78.1 all-gather.11
  418.7 81.4 all-gather.13
  568.5 79.4 all-gather.19

commit v2 on v1

--- a/solution.py
+++ b/solution.py
@@ -14,6 +14,12 @@
     devices = range(lax.axis_size(axis))
     route = [(i - distance, i) for i in devices if i - distance in devices]
     return lax.ppermute(block, axis, route)
+
+
+def gathered_by_exchange(block, axis, concat_axis):
+    count = lax.axis_size(axis)
+    spread = jnp.broadcast_to(block[None], (count,) + block.shape)
+    return lax.all_to_all(spread, axis, split_axis=0, concat_axis=concat_axis + 1, tiled=True)[0]
 
 
 def split3(value):
@@ -80,7 +86,7 @@
             block_starts[jnp.maximum(anchor, 0)],
             fresh_starts[jnp.clip(-anchor - 1, 0, tick_count - 2)],
         )
-        gathered = lax.all_gather(current, "kv", axis=1, tiled=True)
+        gathered = gathered_by_exchange(current, "kv", 1)
         wide = gathered.astype(jnp.float32)
         normed = (
             wide * lax.rsqrt(jnp.mean(wide * wide, axis=1, keepdims=True) + 1e-05) * gain
@@ -88,7 +94,7 @@
         local_cols = jnp.dot(normed, weight_in, preferred_element_type=jnp.float32).astype(
             jnp.bfloat16
         )
-        united = lax.all_gather(local_cols, "kv", axis=1, tiled=True)
+        united = gathered_by_exchange(local_cols, "kv", 1)
         query = united[:, : HEADS_Q * HD].reshape(row_count, KV_HEADS, GROUP, HD)
         new_keys = united[:, HEADS_Q * HD : (HEADS_Q + KV_HEADS) * HD].reshape(
             row_count, KV_HEADS, HD
@@ -142,7 +148,7 @@
         )
         attended = (summed / total[..., None]).reshape(own_rows, HEADS_Q * HD).astype(jnp.bfloat16)
         branch = jnp.dot(
-            lax.all_gather(attended, "kv", axis=0, tiled=True),
+            gathered_by_exchange(attended, "kv", 0),
             weight_out,
             preferred_element_type=jnp.float32,
         )

time: 659 us -> 433 us (0.66)
  waiting for transfers between devices: 531 us -> 78.5 us
  blocking collectives: 0 us -> 230 us
  between operations: 16.6 us -> 3.49 us
    all_gather x6 -> x0, waiting for transfers between devices: 482 us -> none  [the longest x2 165 us: on_device(): gathered = lax.all_gather(current, 'kv', axis=1, tiled=True)]
    all_to_all x0 -> x5, blocking collectives: none -> 230 us  [gathered_by_exchange(): lax.all_to_all(spread, axis, split_axis=0, concat_axis=concat_axis + 1, t...]
    all_to_all x0 -> x1, waiting for transfers between devices: none -> 29 us  [gathered_by_exchange(): lax.all_to_all(spread, axis, split_axis=0, concat_axis=concat_axis + 1, t...]
  transfers between devices with their start and end apart: 9 -> 4, of which waited for: 9 -> 4; matrix products, arithmetic and copies ran while one was open for 2% -> 3% of each run, Pallas kernels for 0% -> 0%
where the time goes in v2:
time: 433 us; the launch traced here: 428 us
  blocking collectives  230 us (53%)
  waiting for transfers between devices  78.5 us (18%)
  local copies, waits for them, and re-layouts  60 us (14%)
  starting transfers between devices  23.7 us (5%)
  other arithmetic  18.2 us (4%)
  matrix products  13.7 us (3%)
    all_to_all x5, blocking collectives, gathered_by_exchange(): lax.all_to_all(spread, axis, split_axis=0, concat_axis=concat_axis + 1, t...  230 us
    all_to_all x2, waiting for transfers between devices, on_device(): lax.all_to_all(packed.reshape(kv_count, own_rows, -1), 'kv', split_axis=0...  48.6 us
    all_to_all x1, waiting for transfers between devices, gathered_by_exchange(): lax.all_to_all(spread, axis, split_axis=0, concat_axis=concat_axis + 1, t...  29 us
    all_to_all x2, starting transfers between devices, on_device(): lax.all_to_all(packed.reshape(kv_count, own_rows, -1), 'kv', split_axis=0...  13.3 us
    concatenate x2, local copies, waits for them, and re-layouts, on_device(): packed = jnp.concatenate([out.astype(jnp.bfloat16)] + split3(lse), axis=1)  9.76 us
  transfers between devices with their start and end apart: 4, of which 4 were waited for; matrix products, arithmetic and copies ran while one was open for 3% of the time, Pallas kernels for 0%

profile of v2, /device:TPU:1, one launch (start us, length us, event | category | flops | bytes accessed | tf_op | source)
XLA Modules:
  0.0 427.6 jit_solution(8061620884838076134)
XLA Ops:
  0.0 1.0 copy.201
  1.5 62.6 %all_to_all.76 = bf16[64,128,128]{1,2,0:T(8,128)(2,1)S(1)} all-to-all(bf16[64,128,128]{1,2,0:T(8,128)(2,1)S(1)} %broadcast_in_dim.185), channel_id=1, replica_groups=mesh['section'=8,'kv'=64] {'kv'}, dimensions={0} | all-to-all | bytes 4194304 | tf_op jit(solution)/shard_map/all_to_all | solution.py:22
  64.1 1.1 fusion.4
  65.2 1.5 fusion.6
  67.3 1.2 broadcast_in_dim.186
  68.5 6.4 %all-to-all-start.1 = ((bf16[64,128,80]{1,2,0:T(8,128)(2,1)}), bf16[64,128,80]{1,2,0:T(8,128)(2,1)S(1)}, u32[]{:S(2)}, u32[]{:S(2)}) async-start(bf16[64,128,80]{1,2,0:T(8,128)(2,1)} %broadcast_in_dim.186), calls=%async_computation.1 | async-start | bytes 2621440 | tf_op jit(solution)/shard_map/all_to_all | solution.py:22
  76.2 0.8 reshape_squeeze.6
  77.1 0.8 reshape_squeeze.7
  79.9 29.0 %all-to-all-done.1 = bf16[64,128,80]{1,2,0:T(8,128)(2,1)S(1)} async-done(((bf16[64,128,80]{1,2,0:T(8,128)(2,1)}), bf16[64,128,80]{1,2,0:T(8,128)(2,1)S(1)}, u32[]{:S(2)}, u32[]{:S(2)}) %all-to-all-start.1) | async-done | bytes 1310752 | tf_op jit(solution)/shard_map/all_to_all | solution.py:22
  108.9 1.1 copy-done.2
  110.0 1.3 slice.56
  111.9 2.1 select_reduce_fusion.1
  114.0 1.3 fusion.1
  115.4 2.7 select_convert_fusion.1
  118.2 1.7 copy.296
  119.8 1.3 convert_element_type.167
  121.2 0.9 copy.207
  122.0 1.1 reshape.317
  124.0 0.8 copy.211
  124.8 0.8 copy.212
  125.6 4.9 %concatenate.46 = bf16[64,2,4192]{2,1,0:T(2,128)(2,1)} concatenate(bf16[64,2,4096]{2,1,0:T(2,128)(2,1)S(1)} %convert_element_type.167, bf16[64,2,32]{2,1,0:T(2,128)(2,1)S(1)} %copy.210, bf16[64,2,32]{2,1,0:T(2,128)(2,1)S(1)} %copy.211, bf16[64,2,32]{2,1,0:T(2,128)(2,1)S(1)} %copy.212), dimensions={2} | concatenate | bytes 2146304 | tf_op jit(solution)/shard_map/concatenate | solution.py:114
  130.5 6.8 %all-to-all-start.2 = ((bf16[64,2,4192]{2,1,0:T(2,128)(2,1)}), bf16[64,2,4192]{2,1,0:T(2,128)(2,1)S(1)}, u32[]{:S(2)}, u32[]{:S(2)}) async-start(bf16[64,2,4192]{2,1,0:T(2,128)(2,1)} %concatenate.46), calls=%async_computation.2 | async-start | bytes 2162688 | tf_op jit(solution)/shard_map/all_to_all | solution.py:115
  137.5 1.4 dynamic-slice_bitcast_fusion.1
  138.8 1.6 copy.213
  140.4 1.0 fusion.104
  142.7 23.8 %all-to-all-done.2 = bf16[64,2,4192]{2,1,0:T(2,128)(2,1)S(1)} async-done(((bf16[64,2,4192]{2,1,0:T(2,128)(2,1)}), bf16[64,2,4192]{2,1,0:T(2,128)(2,1)S(1)}, u32[]{:S(2)}, u32[]{:S(2)}) %all-to-all-start.2) | async-done | bytes 1073184 | tf_op jit(solution)/shard_map/all_to_all | solution.py:115
  166.4 1.0 copy-done.3
  167.4 2.5 slice_convert_fusion.1
  170.0 3.1 reshape.332
  173.0 1.6 fusion.106
  174.7 1.4 copy.255
  176.1 1.4 copy.254
  178.2 0.8 fusion.102
  179.8 0.9 copy.225
  181.5 1.0 broadcast_in_dim.203
  182.5 34.6 %all_to_all.77 = bf16[64,2,4096]{2,1,0:T(2,128)(2,1)S(1)} all-to-all(bf16[64,2,4096]{2,1,0:T(2,128)(2,1)S(1)} %broadcast_in_dim.203), channel_id=1, replica_groups=mesh['section'=8,'kv'=64] {'kv'}, dimensions={0} | all-to-all | bytes 2097152 | tf_op jit(solution)/shard_map/all_to_all | solution.py:22
  217.2 1.2 squeeze.45
  218.4 1.6 fusion.28
  220.1 4.0 collective-permute-start
  224.1 1.0 collective-permute-done
  225.7 58.1 %all_to_all.78 = bf16[64,128,128]{1,2,0:T(8,128)(2,1)S(1)} all-to-all(bf16[64,128,128]{1,2,0:T(8,128)(2,1)S(1)} %broadcast_in_dim.205), channel_id=1, replica_groups=mesh['section'=8,'kv'=64] {'kv'}, dimensions={0} | all-to-all | bytes 4194304 | tf_op jit(solution)/shard_map/all_to_all | solution.py:22
  283.8 1.1 fusion.7
  284.9 1.5 fusion.9
  287.1 39.9 %all_to_all.79 = bf16[64,128,80]{1,2,0:T(8,128)(2,1)S(1)} all-to-all(bf16[64,128,80]{1,2,0:T(8,128)(2,1)S(1)} %broadcast_in_dim.206), channel_id=1, replica_groups=mesh['section'=8,'kv'=64] {'kv'}, dimensions={0} | all-to-all | bytes 2621440 | tf_op jit(solution)/shard_map/all_to_all | solution.py:22
  327.8 2.1 select_reduce_fusion
  329.9 1.3 fusion.3
  331.2 2.7 select_convert_fusion
  334.0 1.7 copy.295
  335.7 1.3 convert_element_type.189
  337.0 0.8 copy.230
  337.8 1.1 reshape.325
  339.4 4.9 %concatenate.53 = bf16[64,2,4192]{2,1,0:T(2,128)(2,1)} concatenate(bf16[64,2,4096]{2,1,0:T(2,128)(2,1)S(1)} %convert_element_type.189, bf16[64,2,32]{2,1,0:T(2,128)(2,1)S(1)} %copy.233, bf16[64,2,32]{2,1,0:T(2,128)(2,1)S(1)} %copy.234, bf16[64,2,32]{2,1,0:T(2,128)(2,1)S(1)} %copy.235), dimensions={2} | concatenate | bytes 2146304 | tf_op jit(solution)/shard_map/concatenate | solution.py:114
  344.3 6.5 %all-to-all-start.6 = ((bf16[64,2,4192]{2,1,0:T(2,128)(2,1)}), bf16[64,2,4192]{2,1,0:T(2,128)(2,1)S(1)}, u32[]{:S(2)}, u32[]{:S(2)}) async-start(bf16[64,2,4192]{2,1,0:T(2,128)(2,1)} %concatenate.53), calls=%async_computation.6 | async-start | bytes 2162688 | tf_op jit(solution)/shard_map/all_to_all | solution.py:115
  350.8 1.4 dynamic-slice_bitcast_fusion
  352.2 1.6 copy.236
  355.1 24.8 %all-to-all-done.6 = bf16[64,2,4192]{2,1,0:T(2,128)(2,1)S(1)} async-done(((bf16[64,2,4192]{2,1,0:T(2,128)(2,1)}), bf16[64,2,4192]{2,1,0:T(2,128)(2,1)S(1)}, u32[]{:S(2)}, u32[]{:S(2)}) %all-to-all-start.6) | async-done | bytes 1073184 | tf_op jit(solution)/shard_map/all_to_all | solution.py:115
  379.9 1.0 copy-done.4
  380.9 2.5 slice_convert_fusion
  383.4 3.1 reshape.334
  386.5 1.0 fusion.105
  388.2 0.7 fusion.23
  389.0 1.0 broadcast_in_dim.209
  390.0 34.8 %all_to_all.80 = bf16[64,2,4096]{2,1,0:T(2,128)(2,1)} all-to-all(bf16[64,2,4096]{2,1,0:T(2,128)(2,1)S(1)} %broadcast_in_dim.209), channel_id=1, replica_groups=mesh['section'=8,'kv'=64] {'kv'}, dimensions={0} | all-to-all | bytes 2097152 | tf_op jit(solution)/shard_map/all_to_all | solution.py:22
  424.8 1.5 squeeze.50
  (111 shorter events, 12.4 us)
Async XLA Ops:
  0.0 66.7 %copy-start = (bf16[1,8192,80]{1,2,0:T(8,128)(2,1)S(1)}, bf16[1,8192,80]{1,2,0:T(8,128)(2,1)}, u32[]{:S(2)}) copy-start(bf16[1,8192,80]{1,2,0:T(8,128)(2,1)} %param.15) | copy-start | bytes 3932164
  1.5 63.7 %copy-start.11 = (f32[1,8192]{1,0:T(1,128)S(1)}, f32[1,8192]{1,0:T(1,128)}, u32[]{:S(2)}) copy-start(f32[1,8192]{1,0:T(1,128)} %param.14) | copy-start | bytes 98308
  67.3 8.9 %copy-start.7 = (bf16[1,384,512]{2,1,0:T(8,128)(2,1)S(1)}, bf16[1,384,512]{2,1,0:T(8,128)(2,1)}, u32[]{:S(2)}) copy-start(bf16[1,384,512]{2,1,0:T(8,128)(2,1)} %param.17) | copy-start | bytes 1179652
  67.3 9.8 %copy-start.8 = (bf16[1,384,512]{2,1,0:T(8,128)(2,1)S(1)}, bf16[1,384,512]{2,1,0:T(8,128)(2,1)}, u32[]{:S(2)}) copy-start(bf16[1,384,512]{2,1,0:T(8,128)(2,1)} %param.18) | copy-start | bytes 1179652
  68.5 9.4 %copy-start.18 = (s32[8]{0:T(128)S(1)}, s32[8]{0:T(128)}, u32[]{:S(2)}) copy-start(s32[8]{0:T(128)} %param.12) | copy-start | bytes 100
  68.5 40.4 %all-to-all-start.1 = ((bf16[64,128,80]{1,2,0:T(8,128)(2,1)}), bf16[64,128,80]{1,2,0:T(8,128)(2,1)S(1)}, u32[]{:S(2)}, u32[]{:S(2)}) async-start(bf16[64,128,80]{1,2,0:T(8,128)(2,1)} %broadcast_in_dim.186), calls=%async_computation.1 | async-start | bytes 2621440 | tf_op jit(solution)/shard_map/all_to_all | solution.py:22
  108.9 1.1 copy-start.2
  114.0 1.4 copy-start.9
  130.5 35.9 %all-to-all-start.2 = ((bf16[64,2,4192]{2,1,0:T(2,128)(2,1)}), bf16[64,2,4192]{2,1,0:T(2,128)(2,1)S(1)}, u32[]{:S(2)}, u32[]{:S(2)}) async-start(bf16[64,2,4192]{2,1,0:T(2,128)(2,1)} %concatenate.46), calls=%async_computation.2 | async-start | bytes 2162688 | tf_op jit(solution)/shard_map/all_to_all | solution.py:115
  137.5 5.0 %copy-start.15 = (pred[16,128]{1,0:T(8,128)(4,1)}, pred[16,128]{1,0:T(8,128)(4,1)S(1)}, u32[]{:S(2)}) copy-start(pred[16,128]{1,0:T(8,128)(4,1)S(1)} %broadcast_in_dim.195) | copy-start | bytes 6148
  166.4 1.0 copy-start.3
  182.5 35.9 %copy-start.5 = (bf16[1,4096,128]{2,1,0:T(8,128)(2,1)S(1)}, bf16[1,4096,128]{2,1,0:T(8,128)(2,1)}, u32[]{:S(2)}) copy-start(bf16[1,4096,128]{2,1,0:T(8,128)(2,1)} %param.16) | copy-start | bytes 3145732
  182.5 35.9 %copy-start.12 = (bf16[1,128,128]{2,1,0:T(8,128)(2,1)S(1)}, bf16[1,128,128]{2,1,0:T(8,128)(2,1)}, u32[]{:S(2)}) copy-start(bf16[1,128,128]{2,1,0:T(8,128)(2,1)} %param.10) | copy-start | bytes 98308
  217.2 7.9 %copy-start.17 = (bf16[1,128,128]{2,1,0:T(8,128)(2,1)S(1)}, bf16[1,128,128]{2,1,0:T(8,128)(2,1)}, u32[]{:S(2)}) copy-start(bf16[1,128,128]{2,1,0:T(8,128)(2,1)} %param.11) | copy-start | bytes 98308
  220.1 4.0 copy-start.13
  220.1 5.0 %collective-permute-start = (bf16[128,128]{1,0:T(8,128)(2,1)S(1)}, bf16[128,128]{1,0:T(8,128)(2,1)S(1)}, u32[]{:S(2)}, u32[]{:S(2)}) collective-permute-start(bf16[128,128]{1,0:T(8,128)(2,1)S(1)} %fusion.28), channel_id=1, source_target_pairs={{0,64},{64,128},{128,192},{192,256},{256,320},{320,384},{384,448},... | collective-permute-start | bytes 98312 | tf_op jit(solution)/shard_map/ppermute | solution.py:16
  329.8 1.4 copy-start.10
  344.3 35.6 %all-to-all-start.6 = ((bf16[64,2,4192]{2,1,0:T(2,128)(2,1)}), bf16[64,2,4192]{2,1,0:T(2,128)(2,1)S(1)}, u32[]{:S(2)}, u32[]{:S(2)}) async-start(bf16[64,2,4192]{2,1,0:T(2,128)(2,1)} %concatenate.53), calls=%async_computation.6 | async-start | bytes 2162688 | tf_op jit(solution)/shard_map/all_to_all | solution.py:115
  350.8 3.1 copy-start.16
  379.9 1.0 copy-start.4
  390.0 36.3 %copy-start.6 = (bf16[1,4096,128]{2,1,0:T(8,128)(2,1)S(1)}, bf16[1,4096,128]{2,1,0:T(8,128)(2,1)}, u32[]{:S(2)}) copy-start(bf16[1,4096,128]{2,1,0:T(8,128)(2,1)} %param.16) | copy-start | bytes 3145732
  390.0 37.3 %copy-start.1 = (bf16[1,8192,80]{1,2,0:T(8,128)(2,1)S(1)}, bf16[1,8192,80]{1,2,0:T(8,128)(2,1)}, u32[]{:S(2)}) copy-start(bf16[1,8192,80]{1,2,0:T(8,128)(2,1)} %param.15) | copy-start | bytes 3932164
  424.8 1.9 copy-start.14
